TPU v7x, 512 devices: a whole 4x4x16 slice. The times are simulated.
512 devices in a mesh: node: 8 (over y, x_lo), space: 64 (over z, x_hi, core).
Axes of the slice: x: 4 (x_hi: 2, x_lo: 2; x = x_hi * 2 + x_lo), y: 4, z: 16, core: 2. Of those that a mesh axis runs over, the one named last changes fastest.
Arguments:
- grain_ids: int32 [256, 16, 128], P('space'), may hold values from 0 to 7
- peak_heat: float32 [256, 16, 128], P('space'), may hold values from 0.5 to 1
Outputs:
- node_states: float32 [8, 8, 256, 16, 128], P('node', None, 'space')
All inputs are finite; a program needn't handle non-finite values.
Results may differ from a plain program's by a relative error of at most 0.0001.
Values sent between devices are 32-bit elements; how exact they have to be, the bound alone decides.
No kernel may reach another device: no remote copies, remote signals or barrier semaphores. Data moves between devices by JAX's collectives and lax.ppermute only.
A program may use at most 64 MiB of HBM per device.

v0:
```python
import math
import jax
import jax.numpy as jnp
import numpy as np
from jax import lax
from jax.sharding import PartitionSpec as P

P_SIZE = 8
NODE_DEV = 1
SWEEPS = 3
JACOBI = 2
STEPS = 2
time_step = 0.25
cross_coef = 1.5
base_heat = 0.45
activation = 3.0


def with_halo(block, sides, width):
    for axis, dim in sides:
        count = lax.axis_size(axis)
        forward = [(i, i + 1) for i in range(count - 1)]
        forward.append((count - 1, 0))
        backward = [(target, source) for source, target in forward]
        low = lax.ppermute(
            lax.slice_in_dim(block, block.shape[dim] - width, None, axis=dim), axis, forward
        )
        high = lax.ppermute(lax.slice_in_dim(block, 0, width, axis=dim), axis, backward)
        block = jnp.concatenate([low, block, high], axis=dim)
    return block


def broadcast(block, axis, source):
    block = jnp.where(lax.axis_index(axis) == source, block, jnp.zeros_like(block))
    return lax.psum(block, axis)


def legendre_pair(count, point):
    before = 1.0
    current = point
    for degree in range(2, count + 1):
        following = ((2 * degree - 1) * point * current - (degree - 1) * before) / degree
        before = current
        current = following
    return (current, before)


def radau_value(count, point):
    high, low = legendre_pair(count, point)
    high_prev, low_prev = legendre_pair(count - 1, point)
    value = high - low
    slope_high = count * (point * high - low) / (point * point - 1.0)
    slope_low = (count - 1) * (point * high_prev - low_prev) / (point * point - 1.0)
    return (value, slope_high - slope_low)


def radau_table(count):
    roots = [1.0]
    for index in range(1, count):
        point = math.cos(2.0 * math.pi * index / (2 * count - 1))
        for repeat in range(100):
            value, slope = radau_value(count, point)
            point = point - value / slope
        roots.append(point)
    roots = sorted(roots)
    times_list = [(value + 1.0) / 2.0 for value in roots]
    times_list[-1] = 1.0
    table = []
    for row_index in range(count):
        upper = times_list[row_index]
        row_values = []
        for column in range(count):
            poly = [1.0]
            for other in range(count):
                if other != column:
                    scale = times_list[column] - times_list[other]
                    shifted = [0.0] + poly
                    scaled = [c * times_list[other] for c in poly] + [0.0]
                    poly = [(shifted[i] - scaled[i]) / scale for i in range(len(shifted))]
            integral_value = 0.0
            for power in range(len(poly)):
                integral_value += poly[power] * upper ** (power + 1) / (power + 1)
            row_values.append(integral_value)
        table.append(row_values)
    return (np.array(times_list), np.array(table))


def drive(field):
    squares = field * field
    total = jnp.sum(squares, axis=-4, keepdims=True)
    return -field + squares * field + 2.0 * cross_coef * field * (total - squares)


def near_sum(extended):
    inner = extended[..., 1:-1, :, :]
    result = extended[..., 2:, :, :] + extended[..., :-2, :, :]
    result = result + jnp.roll(inner, -1, -2) + jnp.roll(inner, 1, -2)
    return result + jnp.roll(inner, -1, -1) + jnp.roll(inner, 1, -1)


def heat_mobility(peak, moment):
    middle = 0.5 * time_step * STEPS
    theta = base_heat + (peak - base_heat) * jnp.exp(-(((moment - middle) / middle) ** 2))
    return jnp.exp(activation * (1.0 - 1.0 / theta))


def rate_on(extended, mobility):
    inner = extended[..., 1:-1, :, :]
    return -mobility * (drive(inner) - (near_sum(extended) - 6.0 * inner))


def relax_on(extended, goal, factor):
    inner = extended[..., 1:-1, :, :]
    return (goal + factor * (near_sum(extended) - drive(inner))) / (1.0 + 6.0 * factor)


def on_device(grain_ids, peak_heat):
    total_nodes = lax.axis_size("node") * NODE_DEV
    node_times, table = radau_table(total_nodes)
    weights = jnp.asarray(table, jnp.float32)
    first = lax.axis_index("node") * NODE_DEV
    times = lax.dynamic_slice_in_dim(jnp.asarray(node_times, jnp.float32), first, NODE_DEV, 0)
    my_rows = lax.dynamic_slice_in_dim(weights, first, NODE_DEV, 0)
    taus = times.reshape((NODE_DEV, 1, 1, 1, 1))
    orders = jnp.arange(P_SIZE, dtype=jnp.int32)
    start = (grain_ids[None] == orders[:, None, None, None]).astype(jnp.float32)
    states = None
    for step_index in range(STEPS):
        moments = (step_index + times) * time_step
        mobility = heat_mobility(peak_heat[None], moments[:, None, None, None])[:, None]
        factor = time_step * taus * mobility
        start_wide = with_halo(start, (("space", 1),), 1)
        rates = rate_on(start_wide[None], mobility)
        states = jnp.broadcast_to(start[None], rates.shape)
        for sweep_index in range(SWEEPS):
            piece = lax.all_gather(rates, "node", axis=0, tiled=True)
            coefs = lax.slice_in_dim(my_rows, 0, piece.shape[0], axis=1)
            quad = jnp.zeros_like(rates) + jnp.tensordot(
                coefs, piece, axes=1, precision=lax.Precision.HIGHEST
            )
            goal = start[None] + time_step * quad - time_step * taus * rates
            last = sweep_index + 1 == SWEEPS
            passes = JACOBI if last else JACOBI + 1
            for relax_index in range(passes):
                extended = with_halo(states, (("space", 2),), 1)
                if relax_index < JACOBI:
                    states = relax_on(extended, goal, factor)
                else:
                    rates = rate_on(extended, mobility)
        if step_index + 1 < STEPS:
            start = broadcast(states[-1], "node", lax.axis_size("node") - 1)
    return states


def solution(mesh):
    in_specs = (P("space", None, None), P("space", None, None))
    out_specs = P("node", None, "space", None, None)
    return jax.shard_map(
        on_device, mesh=mesh, in_specs=in_specs, out_specs=out_specs, check_vma=False
    )
```

profile of v0, /device:TPU:8, one launch (start us, length us, event | category | flops | bytes accessed | tf_op | source)
XLA Modules:
  0.0 647.7 jit_solution(4075357415516616793)
XLA Ops:
  9.3 13.3 %collective-permute-start.1 = (f32[8,1,16,128]{3,2,1,0:T(8,128)S(1)}, f32[8,1,16,128]{3,2,1,0:T(8,128)S(1)}, u32[]{:S(2)}, u32[]{:S(2)}) collective-permute-start(f32[8,1,16,128]{3,2,1,0:T(8,128)S(1)} %get-tuple-element.166), channel_id=1, source_target_pairs={{1,0},{2,1},{3,2},{4,3},{5,4},{6,5},{7,6},{8,7},{9,8},{10,9},{11,1... | collective-permute-start | bytes 196616 | tf_op jit(solution)/shard_map/ppermute | solution.py:28
  27.6 5.7 collective-permute-start.2
  35.7 47.7 %all-gather.7.cloned.1.call-done = f32[8,8,4,16,128]{4,3,2,1,0:T(8,128)} async-done(((f32[1,8,4,16,128]{4,3,2,1,0:T(8,128)}), f32[8,8,4,16,128]{4,3,2,1,0:T(8,128)}) %all-gather.7.cloned.1.call-update) | async-done | bytes 2097168 | tf_op jit(solution)/shard_map/all_gather | solution.py:136
  83.4 4.4 fusion.10
  88.6 7.5 %collective-permute-start.4 = (f32[1,8,1,16,128]{4,3,2,1,0:T(8,128)S(1)}, f32[1,8,1,16,128]{4,3,2,1,0:T(8,128)S(1)}, u32[]{:S(2)}, u32[]{:S(2)}) collective-permute-start(f32[1,8,1,16,128]{4,3,2,1,0:T(8,128)S(1)} %get-tuple-element.155), channel_id=1, source_target_pairs={{1,0},{2,1},{3,2},{4,3},{5,4},{6,5},{7,6},{8,7},{9,8},{10,9},{11,1... | collective-permute-start | bytes 196616 | tf_op jit(solution)/shard_map/ppermute | solution.py:28
  98.1 7.2 %collective-permute-done.5 = f32[1,8,1,16,128]{4,3,2,1,0:T(8,128)S(1)} collective-permute-done((f32[1,8,1,16,128]{4,3,2,1,0:T(8,128)S(1)}, f32[1,8,1,16,128]{4,3,2,1,0:T(8,128)S(1)}, u32[]{:S(2)}, u32[]{:S(2)}) %collective-permute-start.5) | collective-permute-done | bytes 65568 | tf_op jit(solution)/shard_map/ppermute | solution.py:25
  110.4 6.7 %collective-permute-done.7 = f32[1,8,1,16,128]{4,3,2,1,0:T(8,128)S(1)} collective-permute-done((f32[1,8,1,16,128]{4,3,2,1,0:T(8,128)S(1)}, f32[1,8,1,16,128]{4,3,2,1,0:T(8,128)S(1)}, u32[]{:S(2)}, u32[]{:S(2)}) %collective-permute-start.7) | collective-permute-done | bytes 65568 | tf_op jit(solution)/shard_map/ppermute | solution.py:25
  118.2 53.8 %all-gather.9.cloned.1.call-done = f32[8,8,4,16,128]{4,3,2,1,0:T(8,128)} async-done(((f32[1,8,4,16,128]{4,3,2,1,0:T(8,128)}), f32[8,8,4,16,128]{4,3,2,1,0:T(8,128)}) %all-gather.9.cloned.1.call-update) | async-done | bytes 2097168 | tf_op jit(solution)/shard_map/all_gather | solution.py:136
  172.1 4.4 fusion.8
  177.1 7.5 %collective-permute-start.8 = (f32[1,8,1,16,128]{4,3,2,1,0:T(8,128)S(1)}, f32[1,8,1,16,128]{4,3,2,1,0:T(8,128)S(1)}, u32[]{:S(2)}, u32[]{:S(2)}) collective-permute-start(f32[1,8,1,16,128]{4,3,2,1,0:T(8,128)S(1)} %get-tuple-element.135), channel_id=1, source_target_pairs={{1,0},{2,1},{3,2},{4,3},{5,4},{6,5},{7,6},{8,7},{9,8},{10,9},{11,1... | collective-permute-start | bytes 196616 | tf_op jit(solution)/shard_map/ppermute | solution.py:28
  186.5 7.2 %collective-permute-done.9 = f32[1,8,1,16,128]{4,3,2,1,0:T(8,128)S(1)} collective-permute-done((f32[1,8,1,16,128]{4,3,2,1,0:T(8,128)S(1)}, f32[1,8,1,16,128]{4,3,2,1,0:T(8,128)S(1)}, u32[]{:S(2)}, u32[]{:S(2)}) %collective-permute-start.9) | collective-permute-done | bytes 65568 | tf_op jit(solution)/shard_map/ppermute | solution.py:25
  198.9 6.7 %collective-permute-done.11 = f32[1,8,1,16,128]{4,3,2,1,0:T(8,128)S(1)} collective-permute-done((f32[1,8,1,16,128]{4,3,2,1,0:T(8,128)S(1)}, f32[1,8,1,16,128]{4,3,2,1,0:T(8,128)S(1)}, u32[]{:S(2)}, u32[]{:S(2)}) %collective-permute-start.11) | collective-permute-done | bytes 65568 | tf_op jit(solution)/shard_map/ppermute | solution.py:25
  206.9 53.6 %all-gather.11.cloned.1.call-done = f32[8,8,4,16,128]{4,3,2,1,0:T(8,128)} async-done(((f32[1,8,4,16,128]{4,3,2,1,0:T(8,128)}), f32[8,8,4,16,128]{4,3,2,1,0:T(8,128)}) %all-gather.11.cloned.1.call-update) | async-done | bytes 2097168 | tf_op jit(solution)/shard_map/all_gather | solution.py:136
  260.5 4.4 fusion.6
  265.5 7.5 %collective-permute-start.12 = (f32[1,8,1,16,128]{4,3,2,1,0:T(8,128)S(1)}, f32[1,8,1,16,128]{4,3,2,1,0:T(8,128)S(1)}, u32[]{:S(2)}, u32[]{:S(2)}) collective-permute-start(f32[1,8,1,16,128]{4,3,2,1,0:T(8,128)S(1)} %get-tuple-element.115), channel_id=1, source_target_pairs={{1,0},{2,1},{3,2},{4,3},{5,4},{6,5},{7,6},{8,7},{9,8},{10,9},{11,1... | collective-permute-start | bytes 196616 | tf_op jit(solution)/shard_map/ppermute | solution.py:28
  275.0 7.2 %collective-permute-done.13 = f32[1,8,1,16,128]{4,3,2,1,0:T(8,128)S(1)} collective-permute-done((f32[1,8,1,16,128]{4,3,2,1,0:T(8,128)S(1)}, f32[1,8,1,16,128]{4,3,2,1,0:T(8,128)S(1)}, u32[]{:S(2)}, u32[]{:S(2)}) %collective-permute-start.13) | collective-permute-done | bytes 65568 | tf_op jit(solution)/shard_map/ppermute | solution.py:25
  283.4 83.6 %all-reduce.2.cloned.1.call-done = f32[8,4,16,128]{3,2,1,0:T(8,128)} async-done(((f32[8,4,16,128]{3,2,1,0:T(8,128)}), f32[8,4,16,128]{3,2,1,0:T(8,128)}) %all-reduce.2.cloned.1.call-update) | async-done | bytes 262160 | tf_op jit(solution)/shard_map/psum | solution.py:35
  369.8 7.3 %collective-permute-start.15 = (f32[8,1,16,128]{3,2,1,0:T(8,128)S(1)}, f32[8,1,16,128]{3,2,1,0:T(8,128)S(1)}, u32[]{:S(2)}, u32[]{:S(2)}) collective-permute-start(f32[8,1,16,128]{3,2,1,0:T(8,128)S(1)} %get-tuple-element.104), channel_id=1, source_target_pairs={{1,0},{2,1},{3,2},{4,3},{5,4},{6,5},{7,6},{8,7},{9,8},{10,9},{11,1... | collective-permute-start | bytes 196616 | tf_op jit(solution)/shard_map/ppermute | solution.py:28
  381.5 7.3 %collective-permute-start.16 = (f32[1,8,1,16,128]{4,3,2,1,0:T(8,128)S(1)}, f32[1,8,1,16,128]{4,3,2,1,0:T(8,128)S(1)}, u32[]{:S(2)}, u32[]{:S(2)}) collective-permute-start(f32[1,8,1,16,128]{4,3,2,1,0:T(8,128)S(1)} %get-tuple-element.105), channel_id=1, source_target_pairs={{1,0},{2,1},{3,2},{4,3},{5,4},{6,5},{7,6},{8,7},{9,8},{10,9},{11,1... | collective-permute-start | bytes 196616 | tf_op jit(solution)/shard_map/ppermute | solution.py:28
  391.1 49.9 %all-gather.13.cloned.1.call-done = f32[8,8,4,16,128]{4,3,2,1,0:T(8,128)} async-done(((f32[1,8,4,16,128]{4,3,2,1,0:T(8,128)}), f32[8,8,4,16,128]{4,3,2,1,0:T(8,128)}) %all-gather.13.cloned.1.call-update) | async-done | bytes 2097168 | tf_op jit(solution)/shard_map/all_gather | solution.py:136
  441.0 4.4 fusion.4
  446.2 7.5 %collective-permute-start.18 = (f32[1,8,1,16,128]{4,3,2,1,0:T(8,128)S(1)}, f32[1,8,1,16,128]{4,3,2,1,0:T(8,128)S(1)}, u32[]{:S(2)}, u32[]{:S(2)}) collective-permute-start(f32[1,8,1,16,128]{4,3,2,1,0:T(8,128)S(1)} %get-tuple-element.93), channel_id=1, source_target_pairs={{1,0},{2,1},{3,2},{4,3},{5,4},{6,5},{7,6},{8,7},{9,8},{10,9},{11,1... | collective-permute-start | bytes 196616 | tf_op jit(solution)/shard_map/ppermute | solution.py:28
  455.7 7.2 %collective-permute-done.19 = f32[1,8,1,16,128]{4,3,2,1,0:T(8,128)S(1)} collective-permute-done((f32[1,8,1,16,128]{4,3,2,1,0:T(8,128)S(1)}, f32[1,8,1,16,128]{4,3,2,1,0:T(8,128)S(1)}, u32[]{:S(2)}, u32[]{:S(2)}) %collective-permute-start.19) | collective-permute-done | bytes 65568 | tf_op jit(solution)/shard_map/ppermute | solution.py:25
  468.0 6.7 %collective-permute-done.21 = f32[1,8,1,16,128]{4,3,2,1,0:T(8,128)S(1)} collective-permute-done((f32[1,8,1,16,128]{4,3,2,1,0:T(8,128)S(1)}, f32[1,8,1,16,128]{4,3,2,1,0:T(8,128)S(1)}, u32[]{:S(2)}, u32[]{:S(2)}) %collective-permute-start.21) | collective-permute-done | bytes 65568 | tf_op jit(solution)/shard_map/ppermute | solution.py:25
  476.0 53.6 %all-gather.15.cloned.1.call-done = f32[8,8,4,16,128]{4,3,2,1,0:T(8,128)} async-done(((f32[1,8,4,16,128]{4,3,2,1,0:T(8,128)}), f32[8,8,4,16,128]{4,3,2,1,0:T(8,128)}) %all-gather.15.cloned.1.call-update) | async-done | bytes 2097168 | tf_op jit(solution)/shard_map/all_gather | solution.py:136
  529.6 4.4 fusion.2
  534.6 7.5 %collective-permute-start.22 = (f32[1,8,1,16,128]{4,3,2,1,0:T(8,128)S(1)}, f32[1,8,1,16,128]{4,3,2,1,0:T(8,128)S(1)}, u32[]{:S(2)}, u32[]{:S(2)}) collective-permute-start(f32[1,8,1,16,128]{4,3,2,1,0:T(8,128)S(1)} %get-tuple-element.73), channel_id=1, source_target_pairs={{1,0},{2,1},{3,2},{4,3},{5,4},{6,5},{7,6},{8,7},{9,8},{10,9},{11,1... | collective-permute-start | bytes 196616 | tf_op jit(solution)/shard_map/ppermute | solution.py:28
  544.1 7.2 %collective-permute-done.23 = f32[1,8,1,16,128]{4,3,2,1,0:T(8,128)S(1)} collective-permute-done((f32[1,8,1,16,128]{4,3,2,1,0:T(8,128)S(1)}, f32[1,8,1,16,128]{4,3,2,1,0:T(8,128)S(1)}, u32[]{:S(2)}, u32[]{:S(2)}) %collective-permute-start.23) | collective-permute-done | bytes 65568 | tf_op jit(solution)/shard_map/ppermute | solution.py:25
  556.4 6.7 %collective-permute-done.25 = f32[1,8,1,16,128]{4,3,2,1,0:T(8,128)S(1)} collective-permute-done((f32[1,8,1,16,128]{4,3,2,1,0:T(8,128)S(1)}, f32[1,8,1,16,128]{4,3,2,1,0:T(8,128)S(1)}, u32[]{:S(2)}, u32[]{:S(2)}) %collective-permute-start.25) | collective-permute-done | bytes 65568 | tf_op jit(solution)/shard_map/ppermute | solution.py:25
  564.2 53.9 %all-gather.17.cloned.1.call-done = f32[8,8,4,16,128]{4,3,2,1,0:T(8,128)} async-done(((f32[1,8,4,16,128]{4,3,2,1,0:T(8,128)}), f32[8,8,4,16,128]{4,3,2,1,0:T(8,128)}) %all-gather.17.cloned.1.call-update) | async-done | bytes 2097168 | tf_op jit(solution)/shard_map/all_gather | solution.py:136
  623.1 7.5 %collective-permute-start.26 = (f32[1,8,1,16,128]{4,3,2,1,0:T(8,128)S(1)}, f32[1,8,1,16,128]{4,3,2,1,0:T(8,128)S(1)}, u32[]{:S(2)}, u32[]{:S(2)}) collective-permute-start(f32[1,8,1,16,128]{4,3,2,1,0:T(8,128)S(1)} %get-tuple-element.61), channel_id=1, source_target_pairs={{1,0},{2,1},{3,2},{4,3},{5,4},{6,5},{7,6},{8,7},{9,8},{10,9},{11,1... | collective-permute-start | bytes 196616 | tf_op jit(solution)/shard_map/ppermute | solution.py:28
  632.6 7.2 %collective-permute-done.27 = f32[1,8,1,16,128]{4,3,2,1,0:T(8,128)S(1)} collective-permute-done((f32[1,8,1,16,128]{4,3,2,1,0:T(8,128)S(1)}, f32[1,8,1,16,128]{4,3,2,1,0:T(8,128)S(1)}, u32[]{:S(2)}, u32[]{:S(2)}) %collective-permute-start.27) | collective-permute-done | bytes 65568 | tf_op jit(solution)/shard_map/ppermute | solution.py:25
  (167 shorter events, 64.3 us)
Async XLA Ops:
  6.5 76.9 %all-gather.7.cloned.1.call-start = ((), (), s32[]{:S(2)}) async-start(), calls=%async_computation | async-start | bytes 2359296 | tf_op jit(solution)/shard_map/all_gather | solution.py:136
  7.3 18.7 %collective-permute-start = (f32[8,1,16,128]{3,2,1,0:T(8,128)S(1)}, f32[8,1,16,128]{3,2,1,0:T(8,128)S(1)}, u32[]{:S(2)}, u32[]{:S(2)}) collective-permute-start(f32[8,1,16,128]{3,2,1,0:T(8,128)S(1)} %get-tuple-element.165), channel_id=1, source_target_pairs={{0,1},{1,2},{2,3},{3,4},{4,5},{5,6},{6,7},{7,8},{8,9},{9,10},{10,1... | collective-permute-start | bytes 196616 | tf_op jit(solution)/shard_map/ppermute | solution.py:25
  9.3 16.8 %collective-permute-start.1 = (f32[8,1,16,128]{3,2,1,0:T(8,128)S(1)}, f32[8,1,16,128]{3,2,1,0:T(8,128)S(1)}, u32[]{:S(2)}, u32[]{:S(2)}) collective-permute-start(f32[8,1,16,128]{3,2,1,0:T(8,128)S(1)} %get-tuple-element.166), channel_id=1, source_target_pairs={{1,0},{2,1},{3,2},{4,3},{5,4},{6,5},{7,6},{8,7},{9,8},{10,9},{11,1... | collective-permute-start | bytes 196616 | tf_op jit(solution)/shard_map/ppermute | solution.py:28
  27.5 144.6 %all-gather.9.cloned.1.call-start = ((), (), s32[]{:S(2)}) async-start(), calls=%async_computation.1 | async-start | bytes 2359296 | tf_op jit(solution)/shard_map/all_gather | solution.py:136
  27.6 60.3 %collective-permute-start.2 = (f32[1,8,1,16,128]{4,3,2,1,0:T(8,128)S(1)}, f32[1,8,1,16,128]{4,3,2,1,0:T(8,128)S(1)}, u32[]{:S(2)}, u32[]{:S(2)}) collective-permute-start(f32[1,8,1,16,128]{4,3,2,1,0:T(8,128)S(1)} %get-tuple-element.167), channel_id=1, source_target_pairs={{1,0},{2,1},{3,2},{4,3},{5,4},{6,5},{7,6},{8,7},{9,8},{10,9},{11,1... | collective-permute-start | bytes 196616 | tf_op jit(solution)/shard_map/ppermute | solution.py:28
  33.3 54.5 %collective-permute-start.3 = (f32[1,8,1,16,128]{4,3,2,1,0:T(8,128)S(1)}, f32[1,8,1,16,128]{4,3,2,1,0:T(8,128)S(1)}, u32[]{:S(2)}, u32[]{:S(2)}) collective-permute-start(f32[1,8,1,16,128]{4,3,2,1,0:T(8,128)S(1)} %get-tuple-element.168), channel_id=1, source_target_pairs={{0,1},{1,2},{2,3},{3,4},{4,5},{5,6},{6,7},{7,8},{8,9},{9,10},{10,1... | collective-permute-start | bytes 196616 | tf_op jit(solution)/shard_map/ppermute | solution.py:25
  88.6 9.5 %collective-permute-start.4 = (f32[1,8,1,16,128]{4,3,2,1,0:T(8,128)S(1)}, f32[1,8,1,16,128]{4,3,2,1,0:T(8,128)S(1)}, u32[]{:S(2)}, u32[]{:S(2)}) collective-permute-start(f32[1,8,1,16,128]{4,3,2,1,0:T(8,128)S(1)} %get-tuple-element.155), channel_id=1, source_target_pairs={{1,0},{2,1},{3,2},{4,3},{5,4},{6,5},{7,6},{8,7},{9,8},{10,9},{11,1... | collective-permute-start | bytes 196616 | tf_op jit(solution)/shard_map/ppermute | solution.py:28
  96.1 9.2 %collective-permute-start.5 = (f32[1,8,1,16,128]{4,3,2,1,0:T(8,128)S(1)}, f32[1,8,1,16,128]{4,3,2,1,0:T(8,128)S(1)}, u32[]{:S(2)}, u32[]{:S(2)}) collective-permute-start(f32[1,8,1,16,128]{4,3,2,1,0:T(8,128)S(1)} %get-tuple-element.156), channel_id=1, source_target_pairs={{0,1},{1,2},{2,3},{3,4},{4,5},{5,6},{6,7},{7,8},{8,9},{9,10},{10,1... | collective-permute-start | bytes 196616 | tf_op jit(solution)/shard_map/ppermute | solution.py:25
  106.0 4.4 collective-permute-start.6
  108.0 9.2 %collective-permute-start.7 = (f32[1,8,1,16,128]{4,3,2,1,0:T(8,128)S(1)}, f32[1,8,1,16,128]{4,3,2,1,0:T(8,128)S(1)}, u32[]{:S(2)}, u32[]{:S(2)}) collective-permute-start(f32[1,8,1,16,128]{4,3,2,1,0:T(8,128)S(1)} %get-tuple-element.146), channel_id=1, source_target_pairs={{0,1},{1,2},{2,3},{3,4},{4,5},{5,6},{6,7},{7,8},{8,9},{9,10},{10,1... | collective-permute-start | bytes 196616 | tf_op jit(solution)/shard_map/ppermute | solution.py:25
  118.2 142.3 %all-gather.11.cloned.1.call-start = ((), (), s32[]{:S(2)}) async-start(), calls=%async_computation.2 | async-start | bytes 2359296 | tf_op jit(solution)/shard_map/all_gather | solution.py:136
  177.1 9.5 %collective-permute-start.8 = (f32[1,8,1,16,128]{4,3,2,1,0:T(8,128)S(1)}, f32[1,8,1,16,128]{4,3,2,1,0:T(8,128)S(1)}, u32[]{:S(2)}, u32[]{:S(2)}) collective-permute-start(f32[1,8,1,16,128]{4,3,2,1,0:T(8,128)S(1)} %get-tuple-element.135), channel_id=1, source_target_pairs={{1,0},{2,1},{3,2},{4,3},{5,4},{6,5},{7,6},{8,7},{9,8},{10,9},{11,1... | collective-permute-start | bytes 196616 | tf_op jit(solution)/shard_map/ppermute | solution.py:28
  184.6 9.2 %collective-permute-start.9 = (f32[1,8,1,16,128]{4,3,2,1,0:T(8,128)S(1)}, f32[1,8,1,16,128]{4,3,2,1,0:T(8,128)S(1)}, u32[]{:S(2)}, u32[]{:S(2)}) collective-permute-start(f32[1,8,1,16,128]{4,3,2,1,0:T(8,128)S(1)} %get-tuple-element.136), channel_id=1, source_target_pairs={{0,1},{1,2},{2,3},{3,4},{4,5},{5,6},{6,7},{7,8},{8,9},{9,10},{10,1... | collective-permute-start | bytes 196616 | tf_op jit(solution)/shard_map/ppermute | solution.py:25
  196.4 9.2 %collective-permute-start.11 = (f32[1,8,1,16,128]{4,3,2,1,0:T(8,128)S(1)}, f32[1,8,1,16,128]{4,3,2,1,0:T(8,128)S(1)}, u32[]{:S(2)}, u32[]{:S(2)}) collective-permute-start(f32[1,8,1,16,128]{4,3,2,1,0:T(8,128)S(1)} %get-tuple-element.126), channel_id=1, source_target_pairs={{0,1},{1,2},{2,3},{3,4},{4,5},{5,6},{6,7},{7,8},{8,9},{9,10},{10,1... | collective-permute-start | bytes 196616 | tf_op jit(solution)/shard_map/ppermute | solution.py:25
  206.7 160.4 %all-reduce.2.cloned.1.call-start = ((), (), s32[]{:S(2)}) async-start(), calls=%async_computation.3 | async-start | bytes 524288 | tf_op jit(solution)/shard_map/psum | solution.py:35
  265.5 9.5 %collective-permute-start.12 = (f32[1,8,1,16,128]{4,3,2,1,0:T(8,128)S(1)}, f32[1,8,1,16,128]{4,3,2,1,0:T(8,128)S(1)}, u32[]{:S(2)}, u32[]{:S(2)}) collective-permute-start(f32[1,8,1,16,128]{4,3,2,1,0:T(8,128)S(1)} %get-tuple-element.115), channel_id=1, source_target_pairs={{1,0},{2,1},{3,2},{4,3},{5,4},{6,5},{7,6},{8,7},{9,8},{10,9},{11,1... | collective-permute-start | bytes 196616 | tf_op jit(solution)/shard_map/ppermute | solution.py:28
  273.0 9.2 %collective-permute-start.13 = (f32[1,8,1,16,128]{4,3,2,1,0:T(8,128)S(1)}, f32[1,8,1,16,128]{4,3,2,1,0:T(8,128)S(1)}, u32[]{:S(2)}, u32[]{:S(2)}) collective-permute-start(f32[1,8,1,16,128]{4,3,2,1,0:T(8,128)S(1)} %get-tuple-element.116), channel_id=1, source_target_pairs={{0,1},{1,2},{2,3},{3,4},{4,5},{5,6},{6,7},{7,8},{8,9},{9,10},{10,1... | collective-permute-start | bytes 196616 | tf_op jit(solution)/shard_map/ppermute | solution.py:25
  283.3 157.7 %all-gather.13.cloned.1.call-start = ((), (), s32[]{:S(2)}) async-start(), calls=%async_computation.4 | async-start | bytes 2359296 | tf_op jit(solution)/shard_map/all_gather | solution.py:136
  367.9 9.2 %collective-permute-start.14 = (f32[8,1,16,128]{3,2,1,0:T(8,128)S(1)}, f32[8,1,16,128]{3,2,1,0:T(8,128)S(1)}, u32[]{:S(2)}, u32[]{:S(2)}) collective-permute-start(f32[8,1,16,128]{3,2,1,0:T(8,128)S(1)} %get-tuple-element.103), channel_id=1, source_target_pairs={{0,1},{1,2},{2,3},{3,4},{4,5},{5,6},{6,7},{7,8},{8,9},{9,10},{10,1... | collective-permute-start | bytes 196616 | tf_op jit(solution)/shard_map/ppermute | solution.py:25
  369.8 9.1 %collective-permute-start.15 = (f32[8,1,16,128]{3,2,1,0:T(8,128)S(1)}, f32[8,1,16,128]{3,2,1,0:T(8,128)S(1)}, u32[]{:S(2)}, u32[]{:S(2)}) collective-permute-start(f32[8,1,16,128]{3,2,1,0:T(8,128)S(1)} %get-tuple-element.104), channel_id=1, source_target_pairs={{1,0},{2,1},{3,2},{4,3},{5,4},{6,5},{7,6},{8,7},{9,8},{10,9},{11,1... | collective-permute-start | bytes 196616 | tf_op jit(solution)/shard_map/ppermute | solution.py:28
  381.4 148.3 %all-gather.15.cloned.1.call-start = ((), (), s32[]{:S(2)}) async-start(), calls=%async_computation.5 | async-start | bytes 2359296 | tf_op jit(solution)/shard_map/all_gather | solution.py:136
  381.5 64.0 %collective-permute-start.16 = (f32[1,8,1,16,128]{4,3,2,1,0:T(8,128)S(1)}, f32[1,8,1,16,128]{4,3,2,1,0:T(8,128)S(1)}, u32[]{:S(2)}, u32[]{:S(2)}) collective-permute-start(f32[1,8,1,16,128]{4,3,2,1,0:T(8,128)S(1)} %get-tuple-element.105), channel_id=1, source_target_pairs={{1,0},{2,1},{3,2},{4,3},{5,4},{6,5},{7,6},{8,7},{9,8},{10,9},{11,1... | collective-permute-start | bytes 196616 | tf_op jit(solution)/shard_map/ppermute | solution.py:28
  388.8 56.7 %collective-permute-start.17 = (f32[1,8,1,16,128]{4,3,2,1,0:T(8,128)S(1)}, f32[1,8,1,16,128]{4,3,2,1,0:T(8,128)S(1)}, u32[]{:S(2)}, u32[]{:S(2)}) collective-permute-start(f32[1,8,1,16,128]{4,3,2,1,0:T(8,128)S(1)} %get-tuple-element.106), channel_id=1, source_target_pairs={{0,1},{1,2},{2,3},{3,4},{4,5},{5,6},{6,7},{7,8},{8,9},{9,10},{10,1... | collective-permute-start | bytes 196616 | tf_op jit(solution)/shard_map/ppermute | solution.py:25
  446.2 9.5 %collective-permute-start.18 = (f32[1,8,1,16,128]{4,3,2,1,0:T(8,128)S(1)}, f32[1,8,1,16,128]{4,3,2,1,0:T(8,128)S(1)}, u32[]{:S(2)}, u32[]{:S(2)}) collective-permute-start(f32[1,8,1,16,128]{4,3,2,1,0:T(8,128)S(1)} %get-tuple-element.93), channel_id=1, source_target_pairs={{1,0},{2,1},{3,2},{4,3},{5,4},{6,5},{7,6},{8,7},{9,8},{10,9},{11,1... | collective-permute-start | bytes 196616 | tf_op jit(solution)/shard_map/ppermute | solution.py:28
  453.7 9.2 %collective-permute-start.19 = (f32[1,8,1,16,128]{4,3,2,1,0:T(8,128)S(1)}, f32[1,8,1,16,128]{4,3,2,1,0:T(8,128)S(1)}, u32[]{:S(2)}, u32[]{:S(2)}) collective-permute-start(f32[1,8,1,16,128]{4,3,2,1,0:T(8,128)S(1)} %get-tuple-element.94), channel_id=1, source_target_pairs={{0,1},{1,2},{2,3},{3,4},{4,5},{5,6},{6,7},{7,8},{8,9},{9,10},{10,1... | collective-permute-start | bytes 196616 | tf_op jit(solution)/shard_map/ppermute | solution.py:25
  465.5 9.2 %collective-permute-start.21 = (f32[1,8,1,16,128]{4,3,2,1,0:T(8,128)S(1)}, f32[1,8,1,16,128]{4,3,2,1,0:T(8,128)S(1)}, u32[]{:S(2)}, u32[]{:S(2)}) collective-permute-start(f32[1,8,1,16,128]{4,3,2,1,0:T(8,128)S(1)} %get-tuple-element.84), channel_id=1, source_target_pairs={{0,1},{1,2},{2,3},{3,4},{4,5},{5,6},{6,7},{7,8},{8,9},{9,10},{10,1... | collective-permute-start | bytes 196616 | tf_op jit(solution)/shard_map/ppermute | solution.py:25
  475.8 142.3 %all-gather.17.cloned.1.call-start = ((), (), s32[]{:S(2)}) async-start(), calls=%async_computation.6 | async-start | bytes 2359296 | tf_op jit(solution)/shard_map/all_gather | solution.py:136
  534.6 9.5 %collective-permute-start.22 = (f32[1,8,1,16,128]{4,3,2,1,0:T(8,128)S(1)}, f32[1,8,1,16,128]{4,3,2,1,0:T(8,128)S(1)}, u32[]{:S(2)}, u32[]{:S(2)}) collective-permute-start(f32[1,8,1,16,128]{4,3,2,1,0:T(8,128)S(1)} %get-tuple-element.73), channel_id=1, source_target_pairs={{1,0},{2,1},{3,2},{4,3},{5,4},{6,5},{7,6},{8,7},{9,8},{10,9},{11,1... | collective-permute-start | bytes 196616 | tf_op jit(solution)/shard_map/ppermute | solution.py:28
  542.1 9.2 %collective-permute-start.23 = (f32[1,8,1,16,128]{4,3,2,1,0:T(8,128)S(1)}, f32[1,8,1,16,128]{4,3,2,1,0:T(8,128)S(1)}, u32[]{:S(2)}, u32[]{:S(2)}) collective-permute-start(f32[1,8,1,16,128]{4,3,2,1,0:T(8,128)S(1)} %get-tuple-element.74), channel_id=1, source_target_pairs={{0,1},{1,2},{2,3},{3,4},{4,5},{5,6},{6,7},{7,8},{8,9},{9,10},{10,1... | collective-permute-start | bytes 196616 | tf_op jit(solution)/shard_map/ppermute | solution.py:25
  554.0 9.2 %collective-permute-start.25 = (f32[1,8,1,16,128]{4,3,2,1,0:T(8,128)S(1)}, f32[1,8,1,16,128]{4,3,2,1,0:T(8,128)S(1)}, u32[]{:S(2)}, u32[]{:S(2)}) collective-permute-start(f32[1,8,1,16,128]{4,3,2,1,0:T(8,128)S(1)} %get-tuple-element.64), channel_id=1, source_target_pairs={{0,1},{1,2},{2,3},{3,4},{4,5},{5,6},{6,7},{7,8},{8,9},{9,10},{10,1... | collective-permute-start | bytes 196616 | tf_op jit(solution)/shard_map/ppermute | solution.py:25
  623.1 9.5 %collective-permute-start.26 = (f32[1,8,1,16,128]{4,3,2,1,0:T(8,128)S(1)}, f32[1,8,1,16,128]{4,3,2,1,0:T(8,128)S(1)}, u32[]{:S(2)}, u32[]{:S(2)}) collective-permute-start(f32[1,8,1,16,128]{4,3,2,1,0:T(8,128)S(1)} %get-tuple-element.61), channel_id=1, source_target_pairs={{1,0},{2,1},{3,2},{4,3},{5,4},{6,5},{7,6},{8,7},{9,8},{10,9},{11,1... | collective-permute-start | bytes 196616 | tf_op jit(solution)/shard_map/ppermute | solution.py:28
  630.6 9.2 %collective-permute-start.27 = (f32[1,8,1,16,128]{4,3,2,1,0:T(8,128)S(1)}, f32[1,8,1,16,128]{4,3,2,1,0:T(8,128)S(1)}, u32[]{:S(2)}, u32[]{:S(2)}) collective-permute-start(f32[1,8,1,16,128]{4,3,2,1,0:T(8,128)S(1)} %get-tuple-element.62), channel_id=1, source_target_pairs={{0,1},{1,2},{2,3},{3,4},{4,5},{5,6},{6,7},{7,8},{8,9},{9,10},{10,1... | collective-permute-start | bytes 196616 | tf_op jit(solution)/shard_map/ppermute | solution.py:25
  (12 other events, 412.0 us)
Sparse Core Ops, SparseCore 0:
  27.6 55.7 all-gather.6
  118.3 53.7 all-gather.8
  206.8 53.7 all-gather.10
  283.5 83.5 all-reduce.1
  381.5 59.4 all-gather.12
  475.9 53.7 all-gather.14
  564.3 53.7 all-gather.16
where the time goes:
time: 649 us; the launch traced here: 648 us
  waiting for transfers between devices  469 us (72%)
  starting transfers between devices  116 us (18%)
  matrix products  26.6 us (4%)
  between operations  16 us (2%)
  other arithmetic  13.8 us (2%)
  local copies, waits for them, and re-layouts  6.91 us (1%)
    all_gather x6, waiting for transfers between devices, on_device(): piece = lax.all_gather(rates, 'node', axis=0, tiled=True)  313 us
    ppermute x14, starting transfers between devices, with_halo(): lax.ppermute(lax.slice_in_dim(block, 0, width, axis=dim), axis, backward)  86.3 us
    psum x1, waiting for transfers between devices, broadcast(): return lax.psum(block, axis)  83.6 us
    ppermute x14, waiting for transfers between devices, with_halo(): lax.ppermute(lax.slice_in_dim(block, block.shape[dim] - width, None, axis...  70.3 us
    ppermute x14, starting transfers between devices, with_halo(): lax.ppermute(lax.slice_in_dim(block, block.shape[dim] - width, None, axis...  28.8 us
    dot_general x6, matrix products, on_device(): jnp.tensordot(coefs, piece, axes=1, precision=lax.Precision.HIGHEST)  26.6 us
  transfers between devices with their start and end apart: 35, of which 18 were waited for; matrix products, arithmetic and copies ran while one was open for 2% of the time, Pallas kernels for 0%

commit v1 on v0

--- a/solution.py
+++ b/solution.py
@@ -4,6 +4,7 @@
 import numpy as np
 from jax import lax
 from jax.sharding import PartitionSpec as P
+from jax.lax import all_gather
 
 P_SIZE = 8
 NODE_DEV = 1
@@ -32,7 +33,7 @@
 
 def broadcast(block, axis, source):
     block = jnp.where(lax.axis_index(axis) == source, block, jnp.zeros_like(block))
-    return lax.psum(block, axis)
+    return all_gather(block, axis).sum(axis=0)
 
 
 def legendre_pair(count, point):

time: 649 us -> 620 us (0.955)
  waiting for transfers between devices: 469 us -> 439 us
    psum x1 -> x0, waiting for transfers between devices: 83.6 us -> none  [broadcast(): return lax.psum(block, axis)]
    all_gather x0 -> x1, waiting for transfers between devices: none -> 53.8 us  [broadcast(): return all_gather(block, axis).sum(axis=0)]
where the time goes in v1:
time: 620 us; the launch traced here: 618 us
  waiting for transfers between devices  439 us (71%)
  starting transfers between devices  116 us (19%)
  matrix products  26.6 us (4%)
  between operations  16 us (3%)
  other arithmetic  14.6 us (2%)
    all_gather x6, waiting for transfers between devices, on_device(): piece = lax.all_gather(rates, 'node', axis=0, tiled=True)  313 us
    ppermute x14, starting transfers between devices, with_halo(): lax.ppermute(lax.slice_in_dim(block, 0, width, axis=dim), axis, backward)  86.6 us
    ppermute x14, waiting for transfers between devices, with_halo(): lax.ppermute(lax.slice_in_dim(block, block.shape[dim] - width, None, axis...  70.3 us
    all_gather x1, waiting for transfers between devices, broadcast(): return all_gather(block, axis).sum(axis=0)  53.8 us
    ppermute x14, starting transfers between devices, with_halo(): lax.ppermute(lax.slice_in_dim(block, block.shape[dim] - width, None, axis...  28.8 us
    dot_general x6, matrix products, on_device(): jnp.tensordot(coefs, piece, axes=1, precision=lax.Precision.HIGHEST)  26.6 us
  transfers between devices with their start and end apart: 35, of which 18 were waited for; matrix products, arithmetic and copies ran while one was open for 2% of the time, Pallas kernels for 0%

profile of v1, /device:TPU:8, one launch (start us, length us, event | category | flops | bytes accessed | tf_op | source)
XLA Modules:
  0.0 618.4 jit_solution(1358860211013787253)
XLA Ops:
  9.3 13.3 %collective-permute-start.1 = (f32[8,1,16,128]{3,2,1,0:T(8,128)S(1)}, f32[8,1,16,128]{3,2,1,0:T(8,128)S(1)}, u32[]{:S(2)}, u32[]{:S(2)}) collective-permute-start(f32[8,1,16,128]{3,2,1,0:T(8,128)S(1)} %get-tuple-element.167), channel_id=1, source_target_pairs={{1,0},{2,1},{3,2},{4,3},{5,4},{6,5},{7,6},{8,7},{9,8},{10,9},{11,1... | collective-permute-start | bytes 196616 | tf_op jit(solution)/shard_map/ppermute | solution.py:29
  27.6 5.7 collective-permute-start.2
  35.7 47.7 %all-gather.8.cloned.1.call-done = f32[8,8,4,16,128]{4,3,2,1,0:T(8,128)} async-done(((f32[1,8,4,16,128]{4,3,2,1,0:T(8,128)}), f32[8,8,4,16,128]{4,3,2,1,0:T(8,128)}) %all-gather.8.cloned.1.call-update) | async-done | bytes 2097168 | tf_op jit(solution)/shard_map/all_gather | solution.py:137
  83.4 4.4 fusion.10
  88.6 7.5 %collective-permute-start.4 = (f32[1,8,1,16,128]{4,3,2,1,0:T(8,128)S(1)}, f32[1,8,1,16,128]{4,3,2,1,0:T(8,128)S(1)}, u32[]{:S(2)}, u32[]{:S(2)}) collective-permute-start(f32[1,8,1,16,128]{4,3,2,1,0:T(8,128)S(1)} %get-tuple-element.156), channel_id=1, source_target_pairs={{1,0},{2,1},{3,2},{4,3},{5,4},{6,5},{7,6},{8,7},{9,8},{10,9},{11,1... | collective-permute-start | bytes 196616 | tf_op jit(solution)/shard_map/ppermute | solution.py:29
  98.1 7.2 %collective-permute-done.5 = f32[1,8,1,16,128]{4,3,2,1,0:T(8,128)S(1)} collective-permute-done((f32[1,8,1,16,128]{4,3,2,1,0:T(8,128)S(1)}, f32[1,8,1,16,128]{4,3,2,1,0:T(8,128)S(1)}, u32[]{:S(2)}, u32[]{:S(2)}) %collective-permute-start.5) | collective-permute-done | bytes 65568 | tf_op jit(solution)/shard_map/ppermute | solution.py:26
  110.4 6.7 %collective-permute-done.7 = f32[1,8,1,16,128]{4,3,2,1,0:T(8,128)S(1)} collective-permute-done((f32[1,8,1,16,128]{4,3,2,1,0:T(8,128)S(1)}, f32[1,8,1,16,128]{4,3,2,1,0:T(8,128)S(1)}, u32[]{:S(2)}, u32[]{:S(2)}) %collective-permute-start.7) | collective-permute-done | bytes 65568 | tf_op jit(solution)/shard_map/ppermute | solution.py:26
  118.2 53.8 %all-gather.10.cloned.1.call-done = f32[8,8,4,16,128]{4,3,2,1,0:T(8,128)} async-done(((f32[1,8,4,16,128]{4,3,2,1,0:T(8,128)}), f32[8,8,4,16,128]{4,3,2,1,0:T(8,128)}) %all-gather.10.cloned.1.call-update) | async-done | bytes 2097168 | tf_op jit(solution)/shard_map/all_gather | solution.py:137
  172.1 4.4 fusion.8
  177.1 7.5 %collective-permute-start.8 = (f32[1,8,1,16,128]{4,3,2,1,0:T(8,128)S(1)}, f32[1,8,1,16,128]{4,3,2,1,0:T(8,128)S(1)}, u32[]{:S(2)}, u32[]{:S(2)}) collective-permute-start(f32[1,8,1,16,128]{4,3,2,1,0:T(8,128)S(1)} %get-tuple-element.136), channel_id=1, source_target_pairs={{1,0},{2,1},{3,2},{4,3},{5,4},{6,5},{7,6},{8,7},{9,8},{10,9},{11,1... | collective-permute-start | bytes 196616 | tf_op jit(solution)/shard_map/ppermute | solution.py:29
  186.5 7.2 %collective-permute-done.9 = f32[1,8,1,16,128]{4,3,2,1,0:T(8,128)S(1)} collective-permute-done((f32[1,8,1,16,128]{4,3,2,1,0:T(8,128)S(1)}, f32[1,8,1,16,128]{4,3,2,1,0:T(8,128)S(1)}, u32[]{:S(2)}, u32[]{:S(2)}) %collective-permute-start.9) | collective-permute-done | bytes 65568 | tf_op jit(solution)/shard_map/ppermute | solution.py:26
  198.9 6.7 %collective-permute-done.11 = f32[1,8,1,16,128]{4,3,2,1,0:T(8,128)S(1)} collective-permute-done((f32[1,8,1,16,128]{4,3,2,1,0:T(8,128)S(1)}, f32[1,8,1,16,128]{4,3,2,1,0:T(8,128)S(1)}, u32[]{:S(2)}, u32[]{:S(2)}) %collective-permute-start.11) | collective-permute-done | bytes 65568 | tf_op jit(solution)/shard_map/ppermute | solution.py:26
  206.9 53.6 %all-gather.12.cloned.1.call-done = f32[8,8,4,16,128]{4,3,2,1,0:T(8,128)} async-done(((f32[1,8,4,16,128]{4,3,2,1,0:T(8,128)}), f32[8,8,4,16,128]{4,3,2,1,0:T(8,128)}) %all-gather.12.cloned.1.call-update) | async-done | bytes 2097168 | tf_op jit(solution)/shard_map/all_gather | solution.py:137
  260.5 4.4 fusion.6
  265.5 7.5 %collective-permute-start.12 = (f32[1,8,1,16,128]{4,3,2,1,0:T(8,128)S(1)}, f32[1,8,1,16,128]{4,3,2,1,0:T(8,128)S(1)}, u32[]{:S(2)}, u32[]{:S(2)}) collective-permute-start(f32[1,8,1,16,128]{4,3,2,1,0:T(8,128)S(1)} %get-tuple-element.116), channel_id=1, source_target_pairs={{1,0},{2,1},{3,2},{4,3},{5,4},{6,5},{7,6},{8,7},{9,8},{10,9},{11,1... | collective-permute-start | bytes 196616 | tf_op jit(solution)/shard_map/ppermute | solution.py:29
  275.0 7.2 %collective-permute-done.13 = f32[1,8,1,16,128]{4,3,2,1,0:T(8,128)S(1)} collective-permute-done((f32[1,8,1,16,128]{4,3,2,1,0:T(8,128)S(1)}, f32[1,8,1,16,128]{4,3,2,1,0:T(8,128)S(1)}, u32[]{:S(2)}, u32[]{:S(2)}) %collective-permute-start.13) | collective-permute-done | bytes 65568 | tf_op jit(solution)/shard_map/ppermute | solution.py:26
  283.4 53.8 %all-gather.14.cloned.1.call-done = f32[8,8,4,16,128]{4,3,2,1,0:T(8,128)} async-done(((f32[1,8,4,16,128]{4,3,2,1,0:T(8,128)}), f32[8,8,4,16,128]{4,3,2,1,0:T(8,128)}) %all-gather.14.cloned.1.call-update) | async-done | bytes 2097168 | tf_op jit(solution)/shard_map/all_gather | solution.py:36
  340.9 7.5 %collective-permute-start.15 = (f32[8,1,16,128]{3,2,1,0:T(8,128)S(1)}, f32[8,1,16,128]{3,2,1,0:T(8,128)S(1)}, u32[]{:S(2)}, u32[]{:S(2)}) collective-permute-start(f32[8,1,16,128]{3,2,1,0:T(8,128)S(1)} %get-tuple-element.105), channel_id=1, source_target_pairs={{1,0},{2,1},{3,2},{4,3},{5,4},{6,5},{7,6},{8,7},{9,8},{10,9},{11,1... | collective-permute-start | bytes 196616 | tf_op jit(solution)/shard_map/ppermute | solution.py:29
  351.8 7.3 %collective-permute-start.16 = (f32[1,8,1,16,128]{4,3,2,1,0:T(8,128)S(1)}, f32[1,8,1,16,128]{4,3,2,1,0:T(8,128)S(1)}, u32[]{:S(2)}, u32[]{:S(2)}) collective-permute-start(f32[1,8,1,16,128]{4,3,2,1,0:T(8,128)S(1)} %get-tuple-element.106), channel_id=1, source_target_pairs={{1,0},{2,1},{3,2},{4,3},{5,4},{6,5},{7,6},{8,7},{9,8},{10,9},{11,1... | collective-permute-start | bytes 196616 | tf_op jit(solution)/shard_map/ppermute | solution.py:29
  361.5 50.3 %all-gather.16.cloned.1.call-done = f32[8,8,4,16,128]{4,3,2,1,0:T(8,128)} async-done(((f32[1,8,4,16,128]{4,3,2,1,0:T(8,128)}), f32[8,8,4,16,128]{4,3,2,1,0:T(8,128)}) %all-gather.16.cloned.1.call-update) | async-done | bytes 2097168 | tf_op jit(solution)/shard_map/all_gather | solution.py:137
  411.7 4.4 fusion.4
  416.9 7.5 %collective-permute-start.18 = (f32[1,8,1,16,128]{4,3,2,1,0:T(8,128)S(1)}, f32[1,8,1,16,128]{4,3,2,1,0:T(8,128)S(1)}, u32[]{:S(2)}, u32[]{:S(2)}) collective-permute-start(f32[1,8,1,16,128]{4,3,2,1,0:T(8,128)S(1)} %get-tuple-element.94), channel_id=1, source_target_pairs={{1,0},{2,1},{3,2},{4,3},{5,4},{6,5},{7,6},{8,7},{9,8},{10,9},{11,1... | collective-permute-start | bytes 196616 | tf_op jit(solution)/shard_map/ppermute | solution.py:29
  426.4 7.2 %collective-permute-done.19 = f32[1,8,1,16,128]{4,3,2,1,0:T(8,128)S(1)} collective-permute-done((f32[1,8,1,16,128]{4,3,2,1,0:T(8,128)S(1)}, f32[1,8,1,16,128]{4,3,2,1,0:T(8,128)S(1)}, u32[]{:S(2)}, u32[]{:S(2)}) %collective-permute-start.19) | collective-permute-done | bytes 65568 | tf_op jit(solution)/shard_map/ppermute | solution.py:26
  438.7 6.7 %collective-permute-done.21 = f32[1,8,1,16,128]{4,3,2,1,0:T(8,128)S(1)} collective-permute-done((f32[1,8,1,16,128]{4,3,2,1,0:T(8,128)S(1)}, f32[1,8,1,16,128]{4,3,2,1,0:T(8,128)S(1)}, u32[]{:S(2)}, u32[]{:S(2)}) %collective-permute-start.21) | collective-permute-done | bytes 65568 | tf_op jit(solution)/shard_map/ppermute | solution.py:26
  446.7 53.6 %all-gather.18.cloned.1.call-done = f32[8,8,4,16,128]{4,3,2,1,0:T(8,128)} async-done(((f32[1,8,4,16,128]{4,3,2,1,0:T(8,128)}), f32[8,8,4,16,128]{4,3,2,1,0:T(8,128)}) %all-gather.18.cloned.1.call-update) | async-done | bytes 2097168 | tf_op jit(solution)/shard_map/all_gather | solution.py:137
  500.3 4.4 fusion.2
  505.3 7.5 %collective-permute-start.22 = (f32[1,8,1,16,128]{4,3,2,1,0:T(8,128)S(1)}, f32[1,8,1,16,128]{4,3,2,1,0:T(8,128)S(1)}, u32[]{:S(2)}, u32[]{:S(2)}) collective-permute-start(f32[1,8,1,16,128]{4,3,2,1,0:T(8,128)S(1)} %get-tuple-element.74), channel_id=1, source_target_pairs={{1,0},{2,1},{3,2},{4,3},{5,4},{6,5},{7,6},{8,7},{9,8},{10,9},{11,1... | collective-permute-start | bytes 196616 | tf_op jit(solution)/shard_map/ppermute | solution.py:29
  514.8 7.2 %collective-permute-done.23 = f32[1,8,1,16,128]{4,3,2,1,0:T(8,128)S(1)} collective-permute-done((f32[1,8,1,16,128]{4,3,2,1,0:T(8,128)S(1)}, f32[1,8,1,16,128]{4,3,2,1,0:T(8,128)S(1)}, u32[]{:S(2)}, u32[]{:S(2)}) %collective-permute-start.23) | collective-permute-done | bytes 65568 | tf_op jit(solution)/shard_map/ppermute | solution.py:26
  527.1 6.7 %collective-permute-done.25 = f32[1,8,1,16,128]{4,3,2,1,0:T(8,128)S(1)} collective-permute-done((f32[1,8,1,16,128]{4,3,2,1,0:T(8,128)S(1)}, f32[1,8,1,16,128]{4,3,2,1,0:T(8,128)S(1)}, u32[]{:S(2)}, u32[]{:S(2)}) %collective-permute-start.25) | collective-permute-done | bytes 65568 | tf_op jit(solution)/shard_map/ppermute | solution.py:26
  534.9 53.9 %all-gather.20.cloned.1.call-done = f32[8,8,4,16,128]{4,3,2,1,0:T(8,128)} async-done(((f32[1,8,4,16,128]{4,3,2,1,0:T(8,128)}), f32[8,8,4,16,128]{4,3,2,1,0:T(8,128)}) %all-gather.20.cloned.1.call-update) | async-done | bytes 2097168 | tf_op jit(solution)/shard_map/all_gather | solution.py:137
  593.8 7.5 %collective-permute-start.26 = (f32[1,8,1,16,128]{4,3,2,1,0:T(8,128)S(1)}, f32[1,8,1,16,128]{4,3,2,1,0:T(8,128)S(1)}, u32[]{:S(2)}, u32[]{:S(2)}) collective-permute-start(f32[1,8,1,16,128]{4,3,2,1,0:T(8,128)S(1)} %get-tuple-element.62), channel_id=1, source_target_pairs={{1,0},{2,1},{3,2},{4,3},{5,4},{6,5},{7,6},{8,7},{9,8},{10,9},{11,1... | collective-permute-start | bytes 196616 | tf_op jit(solution)/shard_map/ppermute | solution.py:29
  603.2 7.2 %collective-permute-done.27 = f32[1,8,1,16,128]{4,3,2,1,0:T(8,128)S(1)} collective-permute-done((f32[1,8,1,16,128]{4,3,2,1,0:T(8,128)S(1)}, f32[1,8,1,16,128]{4,3,2,1,0:T(8,128)S(1)}, u32[]{:S(2)}, u32[]{:S(2)}) %collective-permute-start.27) | collective-permute-done | bytes 65568 | tf_op jit(solution)/shard_map/ppermute | solution.py:26
  (166 shorter events, 64.2 us)
Async XLA Ops:
  6.5 76.9 %all-gather.8.cloned.1.call-start = ((), (), s32[]{:S(2)}) async-start(), calls=%async_computation | async-start | bytes 2359296 | tf_op jit(solution)/shard_map/all_gather | solution.py:137
  7.3 18.7 %collective-permute-start = (f32[8,1,16,128]{3,2,1,0:T(8,128)S(1)}, f32[8,1,16,128]{3,2,1,0:T(8,128)S(1)}, u32[]{:S(2)}, u32[]{:S(2)}) collective-permute-start(f32[8,1,16,128]{3,2,1,0:T(8,128)S(1)} %get-tuple-element.166), channel_id=1, source_target_pairs={{0,1},{1,2},{2,3},{3,4},{4,5},{5,6},{6,7},{7,8},{8,9},{9,10},{10,1... | collective-permute-start | bytes 196616 | tf_op jit(solution)/shard_map/ppermute | solution.py:26
  9.3 16.8 %collective-permute-start.1 = (f32[8,1,16,128]{3,2,1,0:T(8,128)S(1)}, f32[8,1,16,128]{3,2,1,0:T(8,128)S(1)}, u32[]{:S(2)}, u32[]{:S(2)}) collective-permute-start(f32[8,1,16,128]{3,2,1,0:T(8,128)S(1)} %get-tuple-element.167), channel_id=1, source_target_pairs={{1,0},{2,1},{3,2},{4,3},{5,4},{6,5},{7,6},{8,7},{9,8},{10,9},{11,1... | collective-permute-start | bytes 196616 | tf_op jit(solution)/shard_map/ppermute | solution.py:29
  27.5 144.6 %all-gather.10.cloned.1.call-start = ((), (), s32[]{:S(2)}) async-start(), calls=%async_computation.1 | async-start | bytes 2359296 | tf_op jit(solution)/shard_map/all_gather | solution.py:137
  27.6 60.3 %collective-permute-start.2 = (f32[1,8,1,16,128]{4,3,2,1,0:T(8,128)S(1)}, f32[1,8,1,16,128]{4,3,2,1,0:T(8,128)S(1)}, u32[]{:S(2)}, u32[]{:S(2)}) collective-permute-start(f32[1,8,1,16,128]{4,3,2,1,0:T(8,128)S(1)} %get-tuple-element.168), channel_id=1, source_target_pairs={{1,0},{2,1},{3,2},{4,3},{5,4},{6,5},{7,6},{8,7},{9,8},{10,9},{11,1... | collective-permute-start | bytes 196616 | tf_op jit(solution)/shard_map/ppermute | solution.py:29
  33.3 54.5 %collective-permute-start.3 = (f32[1,8,1,16,128]{4,3,2,1,0:T(8,128)S(1)}, f32[1,8,1,16,128]{4,3,2,1,0:T(8,128)S(1)}, u32[]{:S(2)}, u32[]{:S(2)}) collective-permute-start(f32[1,8,1,16,128]{4,3,2,1,0:T(8,128)S(1)} %get-tuple-element.169), channel_id=1, source_target_pairs={{0,1},{1,2},{2,3},{3,4},{4,5},{5,6},{6,7},{7,8},{8,9},{9,10},{10,1... | collective-permute-start | bytes 196616 | tf_op jit(solution)/shard_map/ppermute | solution.py:26
  88.6 9.5 %collective-permute-start.4 = (f32[1,8,1,16,128]{4,3,2,1,0:T(8,128)S(1)}, f32[1,8,1,16,128]{4,3,2,1,0:T(8,128)S(1)}, u32[]{:S(2)}, u32[]{:S(2)}) collective-permute-start(f32[1,8,1,16,128]{4,3,2,1,0:T(8,128)S(1)} %get-tuple-element.156), channel_id=1, source_target_pairs={{1,0},{2,1},{3,2},{4,3},{5,4},{6,5},{7,6},{8,7},{9,8},{10,9},{11,1... | collective-permute-start | bytes 196616 | tf_op jit(solution)/shard_map/ppermute | solution.py:29
  96.1 9.2 %collective-permute-start.5 = (f32[1,8,1,16,128]{4,3,2,1,0:T(8,128)S(1)}, f32[1,8,1,16,128]{4,3,2,1,0:T(8,128)S(1)}, u32[]{:S(2)}, u32[]{:S(2)}) collective-permute-start(f32[1,8,1,16,128]{4,3,2,1,0:T(8,128)S(1)} %get-tuple-element.157), channel_id=1, source_target_pairs={{0,1},{1,2},{2,3},{3,4},{4,5},{5,6},{6,7},{7,8},{8,9},{9,10},{10,1... | collective-permute-start | bytes 196616 | tf_op jit(solution)/shard_map/ppermute | solution.py:26
  106.0 4.4 collective-permute-start.6
  108.0 9.2 %collective-permute-start.7 = (f32[1,8,1,16,128]{4,3,2,1,0:T(8,128)S(1)}, f32[1,8,1,16,128]{4,3,2,1,0:T(8,128)S(1)}, u32[]{:S(2)}, u32[]{:S(2)}) collective-permute-start(f32[1,8,1,16,128]{4,3,2,1,0:T(8,128)S(1)} %get-tuple-element.147), channel_id=1, source_target_pairs={{0,1},{1,2},{2,3},{3,4},{4,5},{5,6},{6,7},{7,8},{8,9},{9,10},{10,1... | collective-permute-start | bytes 196616 | tf_op jit(solution)/shard_map/ppermute | solution.py:26
  118.2 142.3 %all-gather.12.cloned.1.call-start = ((), (), s32[]{:S(2)}) async-start(), calls=%async_computation.2 | async-start | bytes 2359296 | tf_op jit(solution)/shard_map/all_gather | solution.py:137
  177.1 9.5 %collective-permute-start.8 = (f32[1,8,1,16,128]{4,3,2,1,0:T(8,128)S(1)}, f32[1,8,1,16,128]{4,3,2,1,0:T(8,128)S(1)}, u32[]{:S(2)}, u32[]{:S(2)}) collective-permute-start(f32[1,8,1,16,128]{4,3,2,1,0:T(8,128)S(1)} %get-tuple-element.136), channel_id=1, source_target_pairs={{1,0},{2,1},{3,2},{4,3},{5,4},{6,5},{7,6},{8,7},{9,8},{10,9},{11,1... | collective-permute-start | bytes 196616 | tf_op jit(solution)/shard_map/ppermute | solution.py:29
  184.6 9.2 %collective-permute-start.9 = (f32[1,8,1,16,128]{4,3,2,1,0:T(8,128)S(1)}, f32[1,8,1,16,128]{4,3,2,1,0:T(8,128)S(1)}, u32[]{:S(2)}, u32[]{:S(2)}) collective-permute-start(f32[1,8,1,16,128]{4,3,2,1,0:T(8,128)S(1)} %get-tuple-element.137), channel_id=1, source_target_pairs={{0,1},{1,2},{2,3},{3,4},{4,5},{5,6},{6,7},{7,8},{8,9},{9,10},{10,1... | collective-permute-start | bytes 196616 | tf_op jit(solution)/shard_map/ppermute | solution.py:26
  196.4 9.2 %collective-permute-start.11 = (f32[1,8,1,16,128]{4,3,2,1,0:T(8,128)S(1)}, f32[1,8,1,16,128]{4,3,2,1,0:T(8,128)S(1)}, u32[]{:S(2)}, u32[]{:S(2)}) collective-permute-start(f32[1,8,1,16,128]{4,3,2,1,0:T(8,128)S(1)} %get-tuple-element.127), channel_id=1, source_target_pairs={{0,1},{1,2},{2,3},{3,4},{4,5},{5,6},{6,7},{7,8},{8,9},{9,10},{10,1... | collective-permute-start | bytes 196616 | tf_op jit(solution)/shard_map/ppermute | solution.py:26
  206.7 130.5 %all-gather.14.cloned.1.call-start = ((), (), s32[]{:S(2)}) async-start(), calls=%async_computation.3 | async-start | bytes 2359296 | tf_op jit(solution)/shard_map/all_gather | solution.py:36
  265.5 9.5 %collective-permute-start.12 = (f32[1,8,1,16,128]{4,3,2,1,0:T(8,128)S(1)}, f32[1,8,1,16,128]{4,3,2,1,0:T(8,128)S(1)}, u32[]{:S(2)}, u32[]{:S(2)}) collective-permute-start(f32[1,8,1,16,128]{4,3,2,1,0:T(8,128)S(1)} %get-tuple-element.116), channel_id=1, source_target_pairs={{1,0},{2,1},{3,2},{4,3},{5,4},{6,5},{7,6},{8,7},{9,8},{10,9},{11,1... | collective-permute-start | bytes 196616 | tf_op jit(solution)/shard_map/ppermute | solution.py:29
  273.0 9.2 %collective-permute-start.13 = (f32[1,8,1,16,128]{4,3,2,1,0:T(8,128)S(1)}, f32[1,8,1,16,128]{4,3,2,1,0:T(8,128)S(1)}, u32[]{:S(2)}, u32[]{:S(2)}) collective-permute-start(f32[1,8,1,16,128]{4,3,2,1,0:T(8,128)S(1)} %get-tuple-element.117), channel_id=1, source_target_pairs={{0,1},{1,2},{2,3},{3,4},{4,5},{5,6},{6,7},{7,8},{8,9},{9,10},{10,1... | collective-permute-start | bytes 196616 | tf_op jit(solution)/shard_map/ppermute | solution.py:26
  283.3 128.4 %all-gather.16.cloned.1.call-start = ((), (), s32[]{:S(2)}) async-start(), calls=%async_computation.4 | async-start | bytes 2359296 | tf_op jit(solution)/shard_map/all_gather | solution.py:137
  339.0 9.5 %collective-permute-start.14 = (f32[8,1,16,128]{3,2,1,0:T(8,128)S(1)}, f32[8,1,16,128]{3,2,1,0:T(8,128)S(1)}, u32[]{:S(2)}, u32[]{:S(2)}) collective-permute-start(f32[8,1,16,128]{3,2,1,0:T(8,128)S(1)} %get-tuple-element.104), channel_id=1, source_target_pairs={{0,1},{1,2},{2,3},{3,4},{4,5},{5,6},{6,7},{7,8},{8,9},{9,10},{10,1... | collective-permute-start | bytes 196616 | tf_op jit(solution)/shard_map/ppermute | solution.py:26
  340.9 9.4 %collective-permute-start.15 = (f32[8,1,16,128]{3,2,1,0:T(8,128)S(1)}, f32[8,1,16,128]{3,2,1,0:T(8,128)S(1)}, u32[]{:S(2)}, u32[]{:S(2)}) collective-permute-start(f32[8,1,16,128]{3,2,1,0:T(8,128)S(1)} %get-tuple-element.105), channel_id=1, source_target_pairs={{1,0},{2,1},{3,2},{4,3},{5,4},{6,5},{7,6},{8,7},{9,8},{10,9},{11,1... | collective-permute-start | bytes 196616 | tf_op jit(solution)/shard_map/ppermute | solution.py:29
  351.8 148.6 %all-gather.18.cloned.1.call-start = ((), (), s32[]{:S(2)}) async-start(), calls=%async_computation.5 | async-start | bytes 2359296 | tf_op jit(solution)/shard_map/all_gather | solution.py:137
  351.8 64.4 %collective-permute-start.16 = (f32[1,8,1,16,128]{4,3,2,1,0:T(8,128)S(1)}, f32[1,8,1,16,128]{4,3,2,1,0:T(8,128)S(1)}, u32[]{:S(2)}, u32[]{:S(2)}) collective-permute-start(f32[1,8,1,16,128]{4,3,2,1,0:T(8,128)S(1)} %get-tuple-element.106), channel_id=1, source_target_pairs={{1,0},{2,1},{3,2},{4,3},{5,4},{6,5},{7,6},{8,7},{9,8},{10,9},{11,1... | collective-permute-start | bytes 196616 | tf_op jit(solution)/shard_map/ppermute | solution.py:29
  359.1 57.1 %collective-permute-start.17 = (f32[1,8,1,16,128]{4,3,2,1,0:T(8,128)S(1)}, f32[1,8,1,16,128]{4,3,2,1,0:T(8,128)S(1)}, u32[]{:S(2)}, u32[]{:S(2)}) collective-permute-start(f32[1,8,1,16,128]{4,3,2,1,0:T(8,128)S(1)} %get-tuple-element.107), channel_id=1, source_target_pairs={{0,1},{1,2},{2,3},{3,4},{4,5},{5,6},{6,7},{7,8},{8,9},{9,10},{10,1... | collective-permute-start | bytes 196616 | tf_op jit(solution)/shard_map/ppermute | solution.py:26
  416.9 9.5 %collective-permute-start.18 = (f32[1,8,1,16,128]{4,3,2,1,0:T(8,128)S(1)}, f32[1,8,1,16,128]{4,3,2,1,0:T(8,128)S(1)}, u32[]{:S(2)}, u32[]{:S(2)}) collective-permute-start(f32[1,8,1,16,128]{4,3,2,1,0:T(8,128)S(1)} %get-tuple-element.94), channel_id=1, source_target_pairs={{1,0},{2,1},{3,2},{4,3},{5,4},{6,5},{7,6},{8,7},{9,8},{10,9},{11,1... | collective-permute-start | bytes 196616 | tf_op jit(solution)/shard_map/ppermute | solution.py:29
  424.4 9.2 %collective-permute-start.19 = (f32[1,8,1,16,128]{4,3,2,1,0:T(8,128)S(1)}, f32[1,8,1,16,128]{4,3,2,1,0:T(8,128)S(1)}, u32[]{:S(2)}, u32[]{:S(2)}) collective-permute-start(f32[1,8,1,16,128]{4,3,2,1,0:T(8,128)S(1)} %get-tuple-element.95), channel_id=1, source_target_pairs={{0,1},{1,2},{2,3},{3,4},{4,5},{5,6},{6,7},{7,8},{8,9},{9,10},{10,1... | collective-permute-start | bytes 196616 | tf_op jit(solution)/shard_map/ppermute | solution.py:26
  436.2 9.2 %collective-permute-start.21 = (f32[1,8,1,16,128]{4,3,2,1,0:T(8,128)S(1)}, f32[1,8,1,16,128]{4,3,2,1,0:T(8,128)S(1)}, u32[]{:S(2)}, u32[]{:S(2)}) collective-permute-start(f32[1,8,1,16,128]{4,3,2,1,0:T(8,128)S(1)} %get-tuple-element.85), channel_id=1, source_target_pairs={{0,1},{1,2},{2,3},{3,4},{4,5},{5,6},{6,7},{7,8},{8,9},{9,10},{10,1... | collective-permute-start | bytes 196616 | tf_op jit(solution)/shard_map/ppermute | solution.py:26
  446.5 142.3 %all-gather.20.cloned.1.call-start = ((), (), s32[]{:S(2)}) async-start(), calls=%async_computation.6 | async-start | bytes 2359296 | tf_op jit(solution)/shard_map/all_gather | solution.py:137
  505.3 9.5 %collective-permute-start.22 = (f32[1,8,1,16,128]{4,3,2,1,0:T(8,128)S(1)}, f32[1,8,1,16,128]{4,3,2,1,0:T(8,128)S(1)}, u32[]{:S(2)}, u32[]{:S(2)}) collective-permute-start(f32[1,8,1,16,128]{4,3,2,1,0:T(8,128)S(1)} %get-tuple-element.74), channel_id=1, source_target_pairs={{1,0},{2,1},{3,2},{4,3},{5,4},{6,5},{7,6},{8,7},{9,8},{10,9},{11,1... | collective-permute-start | bytes 196616 | tf_op jit(solution)/shard_map/ppermute | solution.py:29
  512.8 9.2 %collective-permute-start.23 = (f32[1,8,1,16,128]{4,3,2,1,0:T(8,128)S(1)}, f32[1,8,1,16,128]{4,3,2,1,0:T(8,128)S(1)}, u32[]{:S(2)}, u32[]{:S(2)}) collective-permute-start(f32[1,8,1,16,128]{4,3,2,1,0:T(8,128)S(1)} %get-tuple-element.75), channel_id=1, source_target_pairs={{0,1},{1,2},{2,3},{3,4},{4,5},{5,6},{6,7},{7,8},{8,9},{9,10},{10,1... | collective-permute-start | bytes 196616 | tf_op jit(solution)/shard_map/ppermute | solution.py:26
  524.7 9.2 %collective-permute-start.25 = (f32[1,8,1,16,128]{4,3,2,1,0:T(8,128)S(1)}, f32[1,8,1,16,128]{4,3,2,1,0:T(8,128)S(1)}, u32[]{:S(2)}, u32[]{:S(2)}) collective-permute-start(f32[1,8,1,16,128]{4,3,2,1,0:T(8,128)S(1)} %get-tuple-element.65), channel_id=1, source_target_pairs={{0,1},{1,2},{2,3},{3,4},{4,5},{5,6},{6,7},{7,8},{8,9},{9,10},{10,1... | collective-permute-start | bytes 196616 | tf_op jit(solution)/shard_map/ppermute | solution.py:26
  593.8 9.5 %collective-permute-start.26 = (f32[1,8,1,16,128]{4,3,2,1,0:T(8,128)S(1)}, f32[1,8,1,16,128]{4,3,2,1,0:T(8,128)S(1)}, u32[]{:S(2)}, u32[]{:S(2)}) collective-permute-start(f32[1,8,1,16,128]{4,3,2,1,0:T(8,128)S(1)} %get-tuple-element.62), channel_id=1, source_target_pairs={{1,0},{2,1},{3,2},{4,3},{5,4},{6,5},{7,6},{8,7},{9,8},{10,9},{11,1... | collective-permute-start | bytes 196616 | tf_op jit(solution)/shard_map/ppermute | solution.py:29
  601.3 9.2 %collective-permute-start.27 = (f32[1,8,1,16,128]{4,3,2,1,0:T(8,128)S(1)}, f32[1,8,1,16,128]{4,3,2,1,0:T(8,128)S(1)}, u32[]{:S(2)}, u32[]{:S(2)}) collective-permute-start(f32[1,8,1,16,128]{4,3,2,1,0:T(8,128)S(1)} %get-tuple-element.63), channel_id=1, source_target_pairs={{0,1},{1,2},{2,3},{3,4},{4,5},{5,6},{6,7},{7,8},{8,9},{9,10},{10,1... | collective-permute-start | bytes 196616 | tf_op jit(solution)/shard_map/ppermute | solution.py:26
  (11 other events, 411.2 us)
Sparse Core Ops, SparseCore 0:
  27.6 55.7 all-gather.7
  118.3 53.7 all-gather.9
  206.8 53.7 all-gather.11
  283.5 53.7 all-gather.13
  351.9 59.8 all-gather.15
  446.6 53.7 all-gather.17
  535.0 53.7 all-gather.19
